TPU v7x, 128 devices: a whole 4x4x4 slice. The times are simulated.
128 devices in a mesh: frow: 16 (over y, z), fcol: 8 (over x, core).
Axes of the slice: x: 4, y: 4, z: 4, core: 2. Of those that a mesh axis runs over, the one named last changes fastest.
Arguments:
- front_orig: float32 [16, 1024, 8, 2048], P('frow', None, 'fcol'), may hold values from -0.1 to 45, as said below
- child_tiles: bfloat16 [8192, 128, 128], P(('frow', 'fcol')), may hold values from -0.25 to 0.25
- tile_target: int32 [8192, 2], P(('frow', 'fcol')), may hold values from 0 to 127, as said below
- tile_rows: int32 [8192, 128], P(('frow', 'fcol')), may hold values from 0 to 127, each once within a row
- tile_cols: int32 [8192, 128], P(('frow', 'fcol')), may hold values from 0 to 127, each once within a row
Outputs:
- front_out: float32 [16, 1024, 8, 2048], P('frow', None, 'fcol')
Inputs may be any that keep to these rules, and one draw needn't show every extreme that they name: `front_orig`: Symmetric; the lower triangle of the front after every tile is added defines a positive definite matrix. `tile_target`: rows come 64 to a device in device order. Column 0 is the owner, frow index times 8 plus fcol index; column 1 the local block on that owner, local block row times 16 plus local block column; the block lies on or below the front's block diagonal. At most 2 tiles of one device go to one owner, and one owner receives exactly 2 from every device.
All inputs are finite; a program needn't handle non-finite values.
Results may differ from a plain program's by a relative error of at most 0.0003.
Values may be sent and summed in bfloat16 or wider, within the bound.
No kernel may reach another device: no remote copies, remote signals or barrier semaphores. Data moves between devices by JAX's collectives and lax.ppermute only.
A program may use at most 128 MiB of HBM per device.

v0:
```python
import jax
import jax.numpy as jnp
from jax import lax
from jax.sharding import PartitionSpec as P

PW = 512
NPANEL = 2
CAP = 2


def as_sent(x):
    return jax.tree.map(lambda a: a.astype(jnp.bfloat16) if a.dtype == jnp.float32 else a, x)


def broadcast(block, axis, source):
    block = jnp.where(lax.axis_index(axis) == source, block, jnp.zeros_like(block))
    return lax.psum(block, axis)


def place_tiles(received):
    tile_block, perm_block, target_block = received
    width = tile_block.shape[-1]
    positions = jnp.arange(width, dtype=jnp.int32)
    row_onehot = (perm_block[:, :, 0, None, :] == positions[:, None]).astype(jnp.bfloat16)
    col_onehot = (perm_block[:, :, 1, None, :] == positions[:, None]).astype(jnp.bfloat16)
    moved = jnp.einsum(
        "abxi,abij->abxj", row_onehot, tile_block, preferred_element_type=jnp.float32
    ).astype(jnp.bfloat16)
    placed = jnp.einsum(
        "abxj,abyj->abxy", moved, col_onehot, preferred_element_type=jnp.float32
    ).astype(jnp.bfloat16)
    return (placed, target_block)


def subtract_product(matrix, row_factor, col_factor):
    product = jnp.dot(
        row_factor,
        col_factor.T,
        precision=lax.Precision.HIGHEST,
        preferred_element_type=jnp.float32,
    )
    return matrix - product


def shards(front_orig, child_tiles, tile_target, tile_rows, tile_cols):
    row_devs = lax.axis_size("frow")
    col_devs = lax.axis_size("fcol")
    owners = row_devs * col_devs
    row_here = lax.axis_index("frow")
    col_here = lax.axis_index("fcol")
    width = child_tiles.shape[1]
    held = child_tiles.shape[0]
    slot_count = owners * CAP
    owner_of = tile_target[:, 0]
    block_of = tile_target[:, 1]
    tile_order = jnp.arange(held, dtype=jnp.int32)
    same_owner = owner_of[:, None] == owner_of[None, :]
    earlier = tile_order[None, :] < tile_order[:, None]
    rank_of = jnp.sum(jnp.where(same_owner & earlier, 1, 0), axis=1).astype(jnp.int32)
    slot_of = owner_of * CAP + rank_of
    slot_match = slot_of[None, :] == jnp.arange(slot_count, dtype=jnp.int32)[:, None]
    source_tile = jnp.sum(jnp.where(slot_match, tile_order[None, :], 0), axis=1)
    filled = jnp.any(slot_match, axis=1)
    send_tiles = jnp.where(
        filled[:, None, None],
        jnp.take(child_tiles, source_tile, axis=0),
        jnp.zeros((), jnp.bfloat16),
    )
    send_perms = jnp.stack(
        [jnp.take(tile_rows, source_tile, axis=0), jnp.take(tile_cols, source_tile, axis=0)], axis=1
    )
    send_blocks = jnp.take(block_of, source_tile, axis=0)
    placed, blocks_in = place_tiles(
        (
            lax.all_to_all(
                send_tiles.reshape(owners, CAP, width, width),
                ("frow", "fcol"),
                split_axis=0,
                concat_axis=0,
                tiled=True,
            ),
            lax.all_to_all(
                send_perms.reshape(owners, CAP, 2, width),
                ("frow", "fcol"),
                split_axis=0,
                concat_axis=0,
                tiled=True,
            ),
            lax.all_to_all(
                send_blocks.reshape(owners, CAP),
                ("frow", "fcol"),
                split_axis=0,
                concat_axis=0,
                tiled=True,
            ),
        )
    )
    local = front_orig[0, :, 0, :]
    row_blocks = local.shape[0] // width
    col_blocks = local.shape[1] // width
    block_ids = jnp.arange(row_blocks * col_blocks, dtype=jnp.int32)
    block_onehot = (blocks_in.reshape(1, slot_count) == block_ids[:, None]).astype(jnp.bfloat16)
    summed = jnp.dot(
        block_onehot, placed.reshape(slot_count, width * width), preferred_element_type=jnp.float32
    )
    added = (
        summed.reshape(row_blocks, col_blocks, width, width)
        .transpose(0, 2, 1, 3)
        .reshape(local.shape)
    )
    matrix = local + added
    local_rows = jnp.arange(local.shape[0], dtype=jnp.int32)
    local_cols = jnp.arange(local.shape[1], dtype=jnp.int32)
    global_rows = (local_rows // width * row_devs + row_here) * width + local_rows % width
    global_cols = (local_cols // width * col_devs + col_here) * width + local_cols % width
    total = NPANEL * PW
    hi = lax.Precision.HIGHEST
    row_panel = lax.all_gather(matrix[:, :width].astype(jnp.bfloat16), "fcol", axis=1, tiled=True)[
        :, :total
    ]
    half = row_devs // col_devs
    perms = []
    for shift in range(half):
        pairs = []
        for src_row in range(row_devs):
            for src_col in range(col_devs):
                part = src_row // col_devs
                dst_row = (part + shift) % half * col_devs + src_col
                dst_col = src_row % col_devs
                pairs.append((src_row * col_devs + src_col, dst_row * col_devs + dst_col))
        perms.append(pairs)
    got = [lax.ppermute(row_panel, ("frow", "fcol"), perm) for perm in perms]
    my_part = row_here // col_devs
    ordered = []
    for part in range(half):
        pick = got[0]
        for shift in range(1, half):
            pick = jnp.where((my_part - shift) % half == part, got[shift], pick)
        if half == 1:
            pick = got[0]
        ordered.append(pick.reshape(row_blocks, width, total))
    col_panel = jnp.stack(ordered, axis=1).reshape(local.shape[1], total)
    corner_blocks = total // width
    first = matrix[:width, :width].astype(jnp.bfloat16)
    every = lax.all_gather(first, ("frow", "fcol"), axis=0, tiled=False)
    every = every.reshape(row_devs, col_devs, width, width)[:corner_blocks, :corner_blocks]
    corner = every.transpose(0, 2, 1, 3).reshape(total, total).astype(jnp.float32)
    rows_all = jnp.concatenate([row_panel, col_panel], axis=0).astype(jnp.float32)
    n_own = local.shape[0]
    factor_full = jnp.zeros((total, total), jnp.float32)
    pieces = []
    eye = jnp.eye(PW, dtype=jnp.float32)
    for panel_idx in range(NPANEL):
        start = panel_idx * PW
        stop = start + PW
        diag_block = corner[start:stop, start:stop]
        symmetric = jnp.tril(diag_block) + jnp.tril(diag_block, -1).T
        factor = jnp.linalg.cholesky(symmetric)
        inverse = lax.linalg.triangular_solve(factor, eye, left_side=True, lower=True)
        factor_full = factor_full.at[start:stop, start:stop].set(factor)
        solved_rows = jnp.dot(
            rows_all[:, start:stop], inverse.T, precision=hi, preferred_element_type=jnp.float32
        )
        pieces.append(solved_rows)
        if stop < total:
            below = jnp.dot(
                corner[stop:, start:stop],
                inverse.T,
                precision=hi,
                preferred_element_type=jnp.float32,
            )
            factor_full = factor_full.at[stop:, start:stop].set(below)
            corner = corner.at[stop:, stop:].add(
                -jnp.dot(below, below.T, precision=hi, preferred_element_type=jnp.float32)
            )
            rows_all = rows_all.at[:, stop:].add(
                -jnp.dot(solved_rows, below.T, precision=hi, preferred_element_type=jnp.float32)
            )
    solved = jnp.concatenate(pieces, axis=1)
    row_factor = solved[:n_own]
    col_factor = solved[n_own:]
    matrix = subtract_product(matrix, row_factor, col_factor)
    in_corner = (global_rows < total)[:, None]
    corner_rows = jnp.take(factor_full, jnp.clip(global_rows, 0, total - 1), axis=0)
    panel_vals = jnp.where(in_corner, corner_rows, row_factor)
    own_part = lax.dynamic_slice_in_dim(panel_vals, col_here * width, width, axis=1)
    matrix = matrix.at[:, :width].set(own_part)
    lower_part = global_rows[:, None] >= global_cols[None, :]
    result = jnp.where(lower_part, matrix, 0.0)
    return result[None, :, None, :]


def solution(mesh):
    return jax.shard_map(
        shards,
        mesh=mesh,
        in_specs=(
            P("frow", None, "fcol", None),
            P(("frow", "fcol"), None, None),
            P(("frow", "fcol"), None),
            P(("frow", "fcol"), None),
            P(("frow", "fcol"), None),
        ),
        out_specs=P("frow", None, "fcol", None),
        check_vma=False,
    )
```

profile of v0, /device:TPU:1, one launch (start us, length us, event | category | flops | bytes accessed | tf_op | source)
XLA Modules:
  0.0 974.5 jit_solution(10013576491422661252)
XLA Ops:
  11.2 11.5 %all-to-all-start = ((s32[128,1,2]{2,1,0:T(1,128)}), s32[128,1,2]{2,1,0:T(1,128)S(1)}, u32[]{:S(2)}, u32[]{:S(2)}) async-start(s32[128,1,2]{2,1,0:T(1,128)} %bitcast.5), calls=%async_computation | async-start | bytes 131072 | tf_op jit(solution)/shard_map/all_to_all | solution.py:89
  63.1 20.7 %copy.55 = f32[1,1024,1,2048]{1,3,2,0:T(8,128)} copy(f32[1,1024,1,2048]{3,2,1,0:T(1,128)} %param.22) | data formatting | bytes 16777216 | tf_op args[0]
  85.3 78.3 %all-to-all-done.2 = bf16[128,2,128,128]{3,2,1,0:T(8,128)(2,1)} async-done(((bf16[128,2,128,128]{3,2,1,0:T(8,128)(2,1)}), bf16[128,2,128,128]{3,2,1,0:T(8,128)(2,1)}, u32[]{:S(2)}, u32[]{:S(2)}) %all-to-all-start.2) | async-done | bytes 8388640 | tf_op jit(solution)/shard_map/all_to_all | solution.py:75
  163.6 13.1 %fusion.8 = bf16[128,2,128,128]{3,2,1,0:T(8,128)(2,1)} fusion(s32[128,2,128]{2,1,0:T(2,128)S(1)} %get-tuple-element.125, bf16[128,2,128,128]{3,2,1,0:T(8,128)(2,1)} %all-to-all-done.2, s32[128,2,128]{2,1,0:T(2,128)S(1)} %get-tuple-element.124), kind=kOutput, calls=%fused_computation.24 | convolution fusion | flops 2164260864 | bytes 17039360 | tf_op jit(solution)/shard_map/abxj,abyj->abxy/dot_general | solution.py:29
  176.8 35.1 %copy.100 = bf16[32,8,128,128]{3,1,2,0:T(8,128)(2,1)} copy(bf16[32,8,128,128]{3,2,1,0:T(8,128)(2,1)} %bitcast.180) | data formatting | bytes 16777216
  211.9 11.9 %copy.59 = bf16[16384,256]{1,0:T(8,128)(2,1)} copy(bf16[16384,256]{0,1:T(8,128)(2,1)} %bitcast.176) | data formatting | bytes 16777216 | tf_op jit(solution)/shard_map/dot_general | solution.py:103
  258.3 28.5 %all-gather.4.cloned.1.call-done = bf16[1024,1024]{0,1:T(8,128)(2,1)} async-done(((bf16[1024,128]{0,1:T(8,128)(2,1)}), bf16[1024,1024]{0,1:T(8,128)(2,1)}) %all-gather.4.cloned.1.call-update) | async-done | bytes 2097168 | tf_op jit(solution)/shard_map/all_gather | solution.py:118
  300.1 37.2 %collective-permute-done.1 = bf16[1024,1024]{0,1:T(8,128)(2,1)} collective-permute-done((bf16[1024,1024]{0,1:T(8,128)(2,1)}, bf16[1024,1024]{0,1:T(8,128)(2,1)}, u32[]{:S(2)}, u32[]{:S(2)}) %collective-permute-start.1) | collective-permute-done | bytes 2097184 | tf_op jit(solution)/shard_map/ppermute | solution.py:132
  337.2 137.8 %collective-permute-done = bf16[1024,1024]{0,1:T(8,128)(2,1)} collective-permute-done((bf16[1024,1024]{0,1:T(8,128)(2,1)}, bf16[1024,1024]{0,1:T(8,128)(2,1)}, u32[]{:S(2)}, u32[]{:S(2)}) %collective-permute-start) | collective-permute-done | bytes 2097184 | tf_op jit(solution)/shard_map/ppermute | solution.py:132
  492.1 29.1 %all-gather.6.cloned.1.call-done = bf16[16384,128]{0,1:T(8,128)(2,1)} async-done(((bf16[128,128]{0,1:T(8,128)(2,1)}), bf16[16384,128]{0,1:T(8,128)(2,1)}) %all-gather.6.cloned.1.call-update) | async-done | bytes 4194320 | tf_op jit(solution)/shard_map/all_gather | solution.py:145
  538.8 11.7 %cholesky.286 = f32[128,128]{1,0:T(8,128)S(1)} custom-call(f32[128,128]{1,0:T(8,128)S(1)} %cholesky.426), custom_call_target="Cholesky" | custom-call | tf_op jit(solution)/shard_map/jit(cholesky)/cholesky | solution.py:158
  550.6 9.8 %custom-call.27 = f32[1,128,128]{1,2,0:T(8,128)S(1)} custom-call(f32[1,128,128]{2,1,0:T(8,128)S(1)} %get-tuple-element.145), custom_call_target="InvertDiagBlocksLowerTriangular" | custom-call | tf_op jit(solution)/shard_map/jit(cholesky)/cholesky | solution.py:158
  563.0 11.7 %cholesky.305 = f32[128,128]{1,0:T(8,128)S(1)} custom-call(f32[128,128]{1,0:T(8,128)S(1)} %cholesky.430), custom_call_target="Cholesky" | custom-call | tf_op jit(solution)/shard_map/jit(cholesky)/cholesky | solution.py:158
  574.8 10.0 %custom-call.28 = f32[1,128,128]{1,2,0:T(8,128)S(1)} custom-call(f32[1,128,128]{2,1,0:T(8,128)S(1)} %get-tuple-element.142), custom_call_target="InvertDiagBlocksLowerTriangular" | custom-call | tf_op jit(solution)/shard_map/jit(cholesky)/cholesky | solution.py:158
  586.3 11.7 %cholesky.326 = f32[128,128]{1,0:T(8,128)S(1)} custom-call(f32[128,128]{1,0:T(8,128)S(1)} %cholesky.435), custom_call_target="Cholesky" | custom-call | tf_op jit(solution)/shard_map/jit(cholesky)/cholesky | solution.py:158
  598.7 9.8 %custom-call.29 = f32[1,128,128]{1,2,0:T(8,128)S(1)} custom-call(f32[1,128,128]{2,1,0:T(8,128)S(1)} %get-tuple-element.139), custom_call_target="InvertDiagBlocksLowerTriangular" | custom-call | tf_op jit(solution)/shard_map/jit(cholesky)/cholesky | solution.py:158
  610.0 12.1 %cholesky.343 = f32[128,128]{1,0:T(8,128)S(1)} custom-call(f32[128,128]{1,0:T(8,128)S(1)} %convolution_subtract_fusion.11), custom_call_target="Cholesky" | custom-call | tf_op jit(solution)/shard_map/jit(cholesky)/cholesky | solution.py:158
  627.0 11.6 %while.10 = (s32[]{:T(128)}, f32[512,512]{1,0:T(8,128)}, s32[4,2]{0,1:T(2,128)S(1)}, f32[4,128,128]{2,1,0:T(8,128)S(1)}, s32[]{:T(128)}) while((s32[]{:T(128)}, f32[512,512]{1,0:T(8,128)}, s32[4,2]{0,1:T(2,128)S(1)}, f32[4,128,128]{2,1,0:T(8,128)S(1)}, s32[]{:T(128)}) %tuple.86), condition=%wide.while_cond.6, body=%wide.while_body.6.sunk | while | flops 2 | bytes 131189 | solution.py:159
  638.6 39.3 %custom-call.30 = f32[4,128,128]{1,2,0:T(8,128)S(1)} custom-call(f32[4,128,128]{2,1,0:T(8,128)S(1)} %get-tuple-element.94), custom_call_target="InvertDiagBlocksLowerTriangular" | custom-call | tf_op jit(solution)/shard_map/triangular_solve/custom-call.3 | solution.py:159
  700.5 11.7 %cholesky.358 = f32[128,128]{1,0:T(8,128)S(1)} custom-call(f32[128,128]{1,0:T(8,128)S(1)} %cholesky.439), custom_call_target="Cholesky" | custom-call | tf_op jit(solution)/shard_map/jit(cholesky)/cholesky | solution.py:158
  713.0 10.0 %custom-call.31 = f32[1,128,128]{1,2,0:T(8,128)S(1)} custom-call(f32[1,128,128]{2,1,0:T(8,128)S(1)} %get-tuple-element.135), custom_call_target="InvertDiagBlocksLowerTriangular" | custom-call | tf_op jit(solution)/shard_map/jit(cholesky)/cholesky | solution.py:158
  726.3 11.7 %cholesky.377 = f32[128,128]{1,0:T(8,128)S(1)} custom-call(f32[128,128]{1,0:T(8,128)S(1)} %cholesky.443), custom_call_target="Cholesky" | custom-call | tf_op jit(solution)/shard_map/jit(cholesky)/cholesky | solution.py:158
  738.7 9.8 %custom-call.32 = f32[1,128,128]{1,2,0:T(8,128)S(1)} custom-call(f32[1,128,128]{2,1,0:T(8,128)S(1)} %get-tuple-element.132), custom_call_target="InvertDiagBlocksLowerTriangular" | custom-call | tf_op jit(solution)/shard_map/jit(cholesky)/cholesky | solution.py:158
  751.6 11.7 %cholesky.398 = f32[128,128]{1,0:T(8,128)S(1)} custom-call(f32[128,128]{1,0:T(8,128)S(1)} %cholesky.448), custom_call_target="Cholesky" | custom-call | tf_op jit(solution)/shard_map/jit(cholesky)/cholesky | solution.py:158
  764.0 10.0 %custom-call.33 = f32[1,128,128]{1,2,0:T(8,128)S(1)} custom-call(f32[1,128,128]{2,1,0:T(8,128)S(1)} %get-tuple-element.129), custom_call_target="InvertDiagBlocksLowerTriangular" | custom-call | tf_op jit(solution)/shard_map/jit(cholesky)/cholesky | solution.py:158
  776.3 11.7 %cholesky.415 = f32[128,128]{1,0:T(8,128)S(1)} custom-call(f32[128,128]{1,0:T(8,128)S(1)} %convolution_subtract_fusion.10), custom_call_target="Cholesky" | custom-call | tf_op jit(solution)/shard_map/jit(cholesky)/cholesky | solution.py:158
  805.6 11.8 %while.11 = (s32[]{:T(128)}, f32[512,512]{1,0:T(8,128)}, s32[4,2]{0,1:T(2,128)S(1)}, f32[4,128,128]{2,1,0:T(8,128)S(1)}, s32[]{:T(128)}) while((s32[]{:T(128)}, f32[512,512]{1,0:T(8,128)}, s32[4,2]{0,1:T(2,128)S(1)}, f32[4,128,128]{2,1,0:T(8,128)S(1)}, s32[]{:T(128)}) %tuple.96), condition=%wide.while_cond.6.clone, body=%wide.while_body.6.clone.sunk | while | flops 2 | bytes 131189 | solution.py:159
  817.4 39.7 %custom-call.34 = f32[4,128,128]{1,2,0:T(8,128)S(1)} custom-call(f32[4,128,128]{2,1,0:T(8,128)S(1)} %get-tuple-element.95), custom_call_target="InvertDiagBlocksLowerTriangular" | custom-call | tf_op jit(solution)/shard_map/triangular_solve/custom-call.3 | solution.py:159
  873.5 21.5 %fusion.149 = f32[3072,512]{1,0:T(8,128)S(1)} fusion(f32[3072,512]{0,1:T(8,128)S(1)} %fusion.21, f32[512,512]{1,0:T(8,128)S(1)} %get-tuple-element.153), kind=kOutput, calls=%fused_computation.282 | convolution fusion | flops 9663676416 | bytes 13631488 | tf_op jit(solution)/shard_map/dot_general | solution.py:177
  895.0 12.4 %fusion.11 = f32[3072,512]{0,1:T(8,128)S(1)} fusion(f32[3072,512]{1,0:T(8,128)S(1)} %fusion.149, bf16[2048,1024]{1,0:T(8,128)(2,1)} %bitcast.179, bf16[1024,1024]{1,0:T(8,128)(2,1)S(1)} %copy-done.3, f32[128,512]{1,0:T(8,128)S(1)} %fusion.86, f32[128,512]{1,0:T(8,128)S(1)} %copy-done.12, f32[128,512]{1,0:T(8,128)S(1)} %copy-done.6, f32[128,512]{1,0:T(8,128)S(1)} %fusion.65), kind=kOutput, calls=%fused_computation.27 | convolution fusion | flops 9673900032 | bytes 19922944 | tf_op jit(solution)/shard_map/dot_general | solution.py:161
  907.5 30.5 %fusion.16 = f32[1024,2048]{0,1:T(8,128)} fusion(f32[1024,2048]{0,1:T(8,128)} %copy.60, f32[1,1024,1,2048]{1,3,2,0:T(8,128)S(1)} %bitcast.174, f32[3072,512]{0,1:T(8,128)S(1)} %fusion.11, f32[3072,512]{0,1:T(8,128)S(1)} %fusion.21), kind=kOutput, calls=%fused_computation.33 | convolution fusion | flops 25777143808 | bytes 37748736 | tf_op jit(solution)/shard_map/dot_general | solution.py:36
  946.8 20.5 %copy.73 = f32[1,1024,1,2048]{3,2,1,0:T(1,128)} copy(f32[1,1024,1,2048]{1,3,2,0:T(8,128)} %select_bitcast_fusion) | data formatting | bytes 16777216 | tf_op jit(solution)/shard_map/broadcast_in_dim | solution.py:190
  (211 shorter events, 234.3 us)
Async XLA Ops:
  6.5 20.5 %copy-start = (bf16[64,128,128]{2,1,0:T(8,128)(2,1)S(1)}, bf16[64,128,128]{2,1,0:T(8,128)(2,1)}, u32[]{:S(2)}) copy-start(bf16[64,128,128]{2,1,0:T(8,128)(2,1)} %param.23) | copy-start | bytes 6291460
  11.2 24.4 %all-to-all-start = ((s32[128,1,2]{2,1,0:T(1,128)}), s32[128,1,2]{2,1,0:T(1,128)S(1)}, u32[]{:S(2)}, u32[]{:S(2)}) async-start(s32[128,1,2]{2,1,0:T(1,128)} %bitcast.5), calls=%async_computation | async-start | bytes 131072 | tf_op jit(solution)/shard_map/all_to_all | solution.py:89
  35.6 20.7 %all-to-all-start.1 = ((s32[128,2,2,128]{3,1,2,0:T(2,128)}), s32[128,2,2,128]{3,1,2,0:T(2,128)S(1)}, u32[]{:S(2)}, u32[]{:S(2)}) async-start(s32[128,2,2,128]{3,1,2,0:T(2,128)} %pad_add_fusion), calls=%async_computation.1 | async-start | bytes 524288 | tf_op jit(solution)/shard_map/all_to_all | solution.py:82
  56.3 107.4 %all-to-all-start.2 = ((bf16[128,2,128,128]{3,2,1,0:T(8,128)(2,1)}), bf16[128,2,128,128]{3,2,1,0:T(8,128)(2,1)}, u32[]{:S(2)}, u32[]{:S(2)}) async-start(bf16[128,2,128,128]{3,2,1,0:T(8,128)(2,1)} %select_select_fusion), calls=%async_computation.2 | async-start | bytes 16777216 | tf_op jit(solution)/shard_map/all_to_all | solution.py:75
  63.0 223.8 %all-gather.4.cloned.1.call-start = ((), (), s32[]{:S(2)}) async-start(), calls=%async_computation.3 | async-start | bytes 2359296 | tf_op jit(solution)/shard_map/all_gather | solution.py:118
  254.1 2.0 copy-start.4
  256.8 264.3 %all-gather.6.cloned.1.call-start = ((), (), s32[]{:S(2)}) async-start(), calls=%async_computation.4 | async-start | bytes 4227072 | tf_op jit(solution)/shard_map/all_gather | solution.py:145
  286.8 50.5 %collective-permute-start.1 = (bf16[1024,1024]{0,1:T(8,128)(2,1)}, bf16[1024,1024]{0,1:T(8,128)(2,1)}, u32[]{:S(2)}, u32[]{:S(2)}) collective-permute-start(bf16[1024,1024]{0,1:T(8,128)(2,1)} %all-gather.4.cloned.1.call-done), channel_id=1, source_target_pairs={{0,0},{1,8},{2,16},{3,24},{4,32},{5,40},{6,48},{7,56},{8,1},{9,9},... | collective-permute-start | bytes 6291464 | tf_op jit(solution)/shard_map/ppermute | solution.py:132
  290.1 184.9 %collective-permute-start = (bf16[1024,1024]{0,1:T(8,128)(2,1)}, bf16[1024,1024]{0,1:T(8,128)(2,1)}, u32[]{:S(2)}, u32[]{:S(2)}) collective-permute-start(bf16[1024,1024]{0,1:T(8,128)(2,1)} %all-gather.4.cloned.1.call-done), channel_id=1, source_target_pairs={{0,64},{1,72},{2,80},{3,88},{4,96},{5,104},{6,112},{7,120},{8,65},... | collective-permute-start | bytes 6291464 | tf_op jit(solution)/shard_map/ppermute | solution.py:132
  533.4 1.9 copy-start.2
  537.8 1.0 copy-start.10
  680.0 9.6 copy-start.7
  680.0 9.6 copy-start.17
  681.8 11.9 %copy-start.13 = (f32[128,512]{1,0:T(8,128)}, f32[128,512]{1,0:T(8,128)S(1)}, u32[]{:S(2)}) copy-start(f32[128,512]{1,0:T(8,128)S(1)} %fusion.93) | copy-start | bytes 786436
  683.9 9.8 %copy-start.16 = (f32[128,512]{1,0:T(8,128)}, f32[128,512]{1,0:T(8,128)S(1)}, u32[]{:S(2)}) copy-start(f32[128,512]{1,0:T(8,128)S(1)} %fusion.92) | copy-start | bytes 786436
  699.5 1.0 copy-start.9
  725.6 0.7 copy-start.18
  751.0 0.7 copy-start.19
  801.6 64.8 %copy-start.8 = (f32[128,512]{1,0:T(8,128)S(1)}, f32[128,512]{1,0:T(8,128)}, u32[]{:S(2)}) copy-start(f32[128,512]{1,0:T(8,128)} %copy-done.7) | copy-start | bytes 786436
  801.6 64.8 %copy-start.14 = (f32[128,512]{1,0:T(8,128)S(1)}, f32[128,512]{1,0:T(8,128)}, u32[]{:S(2)}) copy-start(f32[128,512]{1,0:T(8,128)} %copy-done.13) | copy-start | bytes 786436
  857.1 0.7 copy-start.20
  860.7 5.6 copy-start.5
  863.4 2.9 copy-start.11
  873.4 21.5 %copy-start.3 = (bf16[1024,1024]{1,0:T(8,128)(2,1)S(1)}, bf16[1024,1024]{1,0:T(8,128)(2,1)}, u32[]{:S(2)}) copy-start(bf16[1024,1024]{1,0:T(8,128)(2,1)} %copy.63) | copy-start | bytes 6291460
  873.4 21.5 %copy-start.6 = (f32[128,512]{1,0:T(8,128)S(1)}, f32[128,512]{1,0:T(8,128)}, u32[]{:S(2)}) copy-start(f32[128,512]{1,0:T(8,128)} %copy-done.5) | copy-start | bytes 786436
  873.5 21.5 %copy-start.12 = (f32[128,512]{1,0:T(8,128)S(1)}, f32[128,512]{1,0:T(8,128)}, u32[]{:S(2)}) copy-start(f32[128,512]{1,0:T(8,128)} %copy-done.11) | copy-start | bytes 786436
  873.5 34.0 %slice-start = ((s8[8388608]{0:T(1024)(128)(4,1)}), s8[4194304]{0:T(1024)(128)(4,1)S(1)}, s32[]{:S(2)}) async-start(s8[8388608]{0:T(1024)(128)(4,1)} %bitcast.173), calls=%async_computation.5 | async-start | bytes 8388608
  895.0 12.4 %slice-start.1 = ((s8[8388608]{0:T(1024)(128)(4,1)}), s8[4194304]{0:T(1024)(128)(4,1)S(1)}, s32[]{:S(2)}) async-start(s8[8388608]{0:T(1024)(128)(4,1)} %bitcast.173), calls=%async_computation.6 | async-start | bytes 8388608
  907.5 30.6 %copy-start.15 = (f32[1024,128]{0,1:T(8,128)S(1)}, f32[1024,128]{0,1:T(8,128)}, u32[]{:S(2)}) copy-start(f32[1024,128]{0,1:T(8,128)} %copy.89) | copy-start | bytes 1572868
  907.5 30.5 %copy-start.21 = (pred[1024]{0:T(1024)(128)(4,1)S(1)}, pred[1024]{0:T(1024)(128)(4,1)}, u32[]{:S(2)}) copy-start(pred[1024]{0:T(1024)(128)(4,1)} %get-tuple-element.158) | copy-start | bytes 3076
  907.5 30.5 %copy-start.22 = (pred[1024]{0:T(1024)(128)(4,1)S(1)}, pred[1024]{0:T(1024)(128)(4,1)}, u32[]{:S(2)}) copy-start(pred[1024]{0:T(1024)(128)(4,1)} %get-tuple-element.159) | copy-start | bytes 3076
  940.8 26.4 %copy-start.1 = (bf16[64,128,128]{2,1,0:T(8,128)(2,1)S(1)}, bf16[64,128,128]{2,1,0:T(8,128)(2,1)}, u32[]{:S(2)}) copy-start(bf16[64,128,128]{2,1,0:T(8,128)(2,1)} %param.23) | copy-start | bytes 6291460
Sparse Core Ops, SparseCore 0:
  256.9 29.7 all-gather.3
  289.6 231.5 all-gather.5
where the time goes:
time: 987 us; the launch traced here: 975 us
  waiting for transfers between devices  314 us (32%)
  other arithmetic  287 us (29%)
  local copies, waits for them, and re-layouts  194 us (20%)
  matrix products  125 us (13%)
  starting transfers between devices  34.3 us (3%)
  between operations  19.6 us (2%)
    ppermute x2, waiting for transfers between devices, shards(): got = [lax.ppermute(row_panel, ('frow', 'fcol'), perm) for perm in perms]  175 us
    another operation x29, other arithmetic, shards(): factor = jnp.linalg.cholesky(symmetric)  158 us
    another operation x4, other arithmetic, shards(): lax.linalg.triangular_solve(factor, eye, left_side=True, lower=True)  80.3 us
    all_to_all x1, waiting for transfers between devices, shards(): lax.all_to_all(send_tiles.reshape(owners, CAP, width, width), ('frow', 'f...  78.3 us
    unnamed x56, local copies, waits for them, and re-layouts  77 us
    dot_general x1, matrix products, subtract_product(): jnp.dot(row_factor, col_factor.T, precision=lax.Precision.HIGHEST, prefer...  30.5 us
    all_gather x1, waiting for transfers between devices, shards(): every = lax.all_gather(first, ('frow', 'fcol'), axis=0, tiled=False)  29.1 us
    all_gather x1, waiting for transfers between devices, shards(): lax.all_gather(matrix[:, :width].astype(jnp.bfloat16), 'fcol', axis=1, ti...  28.5 us
  transfers between devices with their start and end apart: 7, of which 6 were waited for; matrix products, arithmetic and copies ran while one was open for 7% of the time, Pallas kernels for 0%

commit v1 on v0

--- a/solution.py
+++ b/solution.py
@@ -115,9 +115,15 @@
     global_cols = (local_cols // width * col_devs + col_here) * width + local_cols % width
     total = NPANEL * PW
     hi = lax.Precision.HIGHEST
-    row_panel = lax.all_gather(matrix[:, :width].astype(jnp.bfloat16), "fcol", axis=1, tiled=True)[
-        :, :total
-    ]
+    row_panel = jnp.concatenate(
+        lax.all_to_all(
+            jnp.stack([matrix[:, :width].astype(jnp.bfloat16)] * lax.axis_size("fcol")),
+            "fcol",
+            0,
+            0,
+        ),
+        axis=1,
+    )[:, :total]
     half = row_devs // col_devs
     perms = []
     for shift in range(half):

time: 987 us -> 977 us (0.990)
  waiting for transfers between devices: 314 us -> 267 us
  blocking collectives: 0 us -> 34 us
    all_to_all x0 -> x1, blocking collectives: none -> 34 us  [shards(): lax.all_to_all(jnp.stack([matrix[:, :width].astype(jnp.bfloat16)] * lax.a...]
    all_gather x1 -> x0, waiting for transfers between devices: 28.5 us -> none  [shards(): lax.all_gather(matrix[:, :width].astype(jnp.bfloat16), 'fcol', axis=1, ti...]
    all_gather x1, waiting for transfers between devices: 29.1 us -> 10.9 us  [shards(): every = lax.all_gather(first, ('frow', 'fcol'), axis=0, tiled=False)]
  transfers between devices with their start and end apart: 7 -> 6, of which waited for: 6 -> 5; matrix products, arithmetic and copies ran while one was open for 7% -> 7% of each run, Pallas kernels for 0% -> 0%
where the time goes in v1:
time: 977 us; the launch traced here: 964 us
  other arithmetic  287 us (29%)
  waiting for transfers between devices  267 us (27%)
  local copies, waits for them, and re-layouts  195 us (20%)
  matrix products  125 us (13%)
  starting transfers between devices  36.1 us (4%)
  blocking collectives  34 us (3%)
  between operations  19.9 us (2%)
    ppermute x2, waiting for transfers between devices, shards(): got = [lax.ppermute(row_panel, ('frow', 'fcol'), perm) for perm in perms]  175 us
    another operation x29, other arithmetic, shards(): factor = jnp.linalg.cholesky(symmetric)  159 us
    another operation x4, other arithmetic, shards(): lax.linalg.triangular_solve(factor, eye, left_side=True, lower=True)  80.3 us
    all_to_all x1, waiting for transfers between devices, shards(): lax.all_to_all(send_tiles.reshape(owners, CAP, width, width), ('frow', 'f...  78.2 us
    unnamed x56, local copies, waits for them, and re-layouts  77.1 us
    all_to_all x1, blocking collectives, shards(): lax.all_to_all(jnp.stack([matrix[:, :width].astype(jnp.bfloat16)] * lax.a...  34 us
    dot_general x1, matrix products, subtract_product(): jnp.dot(row_factor, col_factor.T, precision=lax.Precision.HIGHEST, prefer...  30.5 us
    another operation x27, local copies, waits for them, and re-layouts, shards(): lax.linalg.triangular_solve(factor, eye, left_side=True, lower=True)  23.6 us
  transfers between devices with their start and end apart: 6, of which 5 were waited for; matrix products, arithmetic and copies ran while one was open for 7% of the time, Pallas kernels for 0%

profile of v1, /device:TPU:1, one launch (start us, length us, event | category | flops | bytes accessed | tf_op | source)
XLA Modules:
  0.0 964.1 jit_solution(17502725451256504966)
XLA Ops:
  11.2 11.5 %all-to-all-start = ((s32[128,1,2]{2,1,0:T(1,128)}), s32[128,1,2]{2,1,0:T(1,128)S(1)}, u32[]{:S(2)}, u32[]{:S(2)}) async-start(s32[128,1,2]{2,1,0:T(1,128)} %bitcast.5), calls=%async_computation | async-start | bytes 131072 | tf_op jit(solution)/shard_map/all_to_all | solution.py:89
  63.1 20.7 %copy.55 = f32[1,1024,1,2048]{1,3,2,0:T(8,128)} copy(f32[1,1024,1,2048]{3,2,1,0:T(1,128)} %param.22) | data formatting | bytes 16777216 | tf_op args[0]
  85.4 78.2 %all-to-all-done.2 = bf16[128,2,128,128]{3,2,1,0:T(8,128)(2,1)} async-done(((bf16[128,2,128,128]{3,2,1,0:T(8,128)(2,1)}), bf16[128,2,128,128]{3,2,1,0:T(8,128)(2,1)}, u32[]{:S(2)}, u32[]{:S(2)}) %all-to-all-start.2) | async-done | bytes 8388640 | tf_op jit(solution)/shard_map/all_to_all | solution.py:75
  163.6 13.1 %fusion.8 = bf16[128,2,128,128]{3,2,1,0:T(8,128)(2,1)} fusion(s32[128,2,128]{2,1,0:T(2,128)S(1)} %get-tuple-element.125, bf16[128,2,128,128]{3,2,1,0:T(8,128)(2,1)} %all-to-all-done.2, s32[128,2,128]{2,1,0:T(2,128)S(1)} %get-tuple-element.124), kind=kOutput, calls=%fused_computation.24 | convolution fusion | flops 2164260864 | bytes 17039360 | tf_op jit(solution)/shard_map/abxj,abyj->abxy/dot_general | solution.py:29
  176.8 35.3 %copy.100 = bf16[32,8,128,128]{3,1,2,0:T(8,128)(2,1)} copy(bf16[32,8,128,128]{3,2,1,0:T(8,128)(2,1)} %bitcast.183) | data formatting | bytes 16777216
  212.0 11.9 %copy.59 = bf16[16384,256]{1,0:T(8,128)(2,1)} copy(bf16[16384,256]{0,1:T(8,128)(2,1)} %bitcast.179) | data formatting | bytes 16777216 | tf_op jit(solution)/shard_map/dot_general | solution.py:103
  258.1 34.0 %all_to_all.21 = bf16[8,1024,128]{1,2,0:T(8,128)(2,1)} all-to-all(bf16[8,1024,128]{1,2,0:T(8,128)(2,1)S(1)} %stack.26), channel_id=1, replica_groups=mesh['frow'=16,'fcol'=8] {'fcol'}, dimensions={0} | all-to-all | bytes 4194304 | tf_op jit(solution)/shard_map/all_to_all | solution.py:119
  307.2 37.9 %collective-permute-done.1 = bf16[1024,1024]{0,1:T(8,128)(2,1)} collective-permute-done((bf16[1024,1024]{0,1:T(8,128)(2,1)}, bf16[1024,1024]{0,1:T(8,128)(2,1)}, u32[]{:S(2)}, u32[]{:S(2)}) %collective-permute-start.1) | collective-permute-done | bytes 2097184 | tf_op jit(solution)/shard_map/ppermute | solution.py:138
  345.1 136.6 %collective-permute-done = bf16[1024,1024]{0,1:T(8,128)(2,1)} collective-permute-done((bf16[1024,1024]{0,1:T(8,128)(2,1)}, bf16[1024,1024]{0,1:T(8,128)(2,1)}, u32[]{:S(2)}, u32[]{:S(2)}) %collective-permute-start) | collective-permute-done | bytes 2097184 | tf_op jit(solution)/shard_map/ppermute | solution.py:138
  498.8 10.9 %all-gather.3.cloned.1.call-done = bf16[16384,128]{0,1:T(8,128)(2,1)} async-done(((bf16[128,128]{0,1:T(8,128)(2,1)}), bf16[16384,128]{0,1:T(8,128)(2,1)}) %all-gather.3.cloned.1.call-update) | async-done | bytes 4194320 | tf_op jit(solution)/shard_map/all_gather | solution.py:151
  527.3 11.7 %cholesky.286 = f32[128,128]{1,0:T(8,128)S(1)} custom-call(f32[128,128]{1,0:T(8,128)S(1)} %cholesky.426), custom_call_target="Cholesky" | custom-call | tf_op jit(solution)/shard_map/jit(cholesky)/cholesky | solution.py:164
  539.1 9.8 %custom-call.27 = f32[1,128,128]{1,2,0:T(8,128)S(1)} custom-call(f32[1,128,128]{2,1,0:T(8,128)S(1)} %get-tuple-element.145), custom_call_target="InvertDiagBlocksLowerTriangular" | custom-call | tf_op jit(solution)/shard_map/jit(cholesky)/cholesky | solution.py:164
  551.6 11.7 %cholesky.305 = f32[128,128]{1,0:T(8,128)S(1)} custom-call(f32[128,128]{1,0:T(8,128)S(1)} %cholesky.430), custom_call_target="Cholesky" | custom-call | tf_op jit(solution)/shard_map/jit(cholesky)/cholesky | solution.py:164
  563.3 10.0 %custom-call.28 = f32[1,128,128]{1,2,0:T(8,128)S(1)} custom-call(f32[1,128,128]{2,1,0:T(8,128)S(1)} %get-tuple-element.142), custom_call_target="InvertDiagBlocksLowerTriangular" | custom-call | tf_op jit(solution)/shard_map/jit(cholesky)/cholesky | solution.py:164
  574.8 11.7 %cholesky.326 = f32[128,128]{1,0:T(8,128)S(1)} custom-call(f32[128,128]{1,0:T(8,128)S(1)} %cholesky.435), custom_call_target="Cholesky" | custom-call | tf_op jit(solution)/shard_map/jit(cholesky)/cholesky | solution.py:164
  587.3 9.8 %custom-call.29 = f32[1,128,128]{1,2,0:T(8,128)S(1)} custom-call(f32[1,128,128]{2,1,0:T(8,128)S(1)} %get-tuple-element.139), custom_call_target="InvertDiagBlocksLowerTriangular" | custom-call | tf_op jit(solution)/shard_map/jit(cholesky)/cholesky | solution.py:164
  598.5 12.1 %cholesky.343 = f32[128,128]{1,0:T(8,128)S(1)} custom-call(f32[128,128]{1,0:T(8,128)S(1)} %convolution_subtract_fusion.11), custom_call_target="Cholesky" | custom-call | tf_op jit(solution)/shard_map/jit(cholesky)/cholesky | solution.py:164
  615.9 11.9 %while.10 = (s32[]{:T(128)}, f32[512,512]{1,0:T(8,128)}, s32[4,2]{0,1:T(2,128)S(1)}, f32[4,128,128]{2,1,0:T(8,128)S(1)}, s32[]{:T(128)}) while((s32[]{:T(128)}, f32[512,512]{1,0:T(8,128)}, s32[4,2]{0,1:T(2,128)S(1)}, f32[4,128,128]{2,1,0:T(8,128)S(1)}, s32[]{:T(128)}) %tuple.86), condition=%wide.while_cond.6, body=%wide.while_body.6.sunk | while | flops 2 | bytes 131189 | solution.py:165
  627.7 39.3 %custom-call.30 = f32[4,128,128]{1,2,0:T(8,128)S(1)} custom-call(f32[4,128,128]{2,1,0:T(8,128)S(1)} %get-tuple-element.94), custom_call_target="InvertDiagBlocksLowerTriangular" | custom-call | tf_op jit(solution)/shard_map/triangular_solve/custom-call.3 | solution.py:165
  689.7 11.7 %cholesky.358 = f32[128,128]{1,0:T(8,128)S(1)} custom-call(f32[128,128]{1,0:T(8,128)S(1)} %cholesky.439), custom_call_target="Cholesky" | custom-call | tf_op jit(solution)/shard_map/jit(cholesky)/cholesky | solution.py:164
  702.2 10.0 %custom-call.31 = f32[1,128,128]{1,2,0:T(8,128)S(1)} custom-call(f32[1,128,128]{2,1,0:T(8,128)S(1)} %get-tuple-element.135), custom_call_target="InvertDiagBlocksLowerTriangular" | custom-call | tf_op jit(solution)/shard_map/jit(cholesky)/cholesky | solution.py:164
  715.5 11.7 %cholesky.377 = f32[128,128]{1,0:T(8,128)S(1)} custom-call(f32[128,128]{1,0:T(8,128)S(1)} %cholesky.443), custom_call_target="Cholesky" | custom-call | tf_op jit(solution)/shard_map/jit(cholesky)/cholesky | solution.py:164
  727.9 9.8 %custom-call.32 = f32[1,128,128]{1,2,0:T(8,128)S(1)} custom-call(f32[1,128,128]{2,1,0:T(8,128)S(1)} %get-tuple-element.132), custom_call_target="InvertDiagBlocksLowerTriangular" | custom-call | tf_op jit(solution)/shard_map/jit(cholesky)/cholesky | solution.py:164
  740.9 11.7 %cholesky.398 = f32[128,128]{1,0:T(8,128)S(1)} custom-call(f32[128,128]{1,0:T(8,128)S(1)} %cholesky.448), custom_call_target="Cholesky" | custom-call | tf_op jit(solution)/shard_map/jit(cholesky)/cholesky | solution.py:164
  753.3 10.0 %custom-call.33 = f32[1,128,128]{1,2,0:T(8,128)S(1)} custom-call(f32[1,128,128]{2,1,0:T(8,128)S(1)} %get-tuple-element.129), custom_call_target="InvertDiagBlocksLowerTriangular" | custom-call | tf_op jit(solution)/shard_map/jit(cholesky)/cholesky | solution.py:164
  765.6 11.7 %cholesky.415 = f32[128,128]{1,0:T(8,128)S(1)} custom-call(f32[128,128]{1,0:T(8,128)S(1)} %convolution_subtract_fusion.10), custom_call_target="Cholesky" | custom-call | tf_op jit(solution)/shard_map/jit(cholesky)/cholesky | solution.py:164
  795.1 11.8 %while.11 = (s32[]{:T(128)}, f32[512,512]{1,0:T(8,128)}, s32[4,2]{0,1:T(2,128)S(1)}, f32[4,128,128]{2,1,0:T(8,128)S(1)}, s32[]{:T(128)}) while((s32[]{:T(128)}, f32[512,512]{1,0:T(8,128)}, s32[4,2]{0,1:T(2,128)S(1)}, f32[4,128,128]{2,1,0:T(8,128)S(1)}, s32[]{:T(128)}) %tuple.94), condition=%wide.while_cond.6.clone, body=%wide.while_body.6.clone.sunk | while | flops 2 | bytes 131189 | solution.py:165
  806.9 39.7 %custom-call.34 = f32[4,128,128]{1,2,0:T(8,128)S(1)} custom-call(f32[4,128,128]{2,1,0:T(8,128)S(1)} %get-tuple-element.95), custom_call_target="InvertDiagBlocksLowerTriangular" | custom-call | tf_op jit(solution)/shard_map/triangular_solve/custom-call.3 | solution.py:165
  863.0 21.5 %fusion.149 = f32[3072,512]{1,0:T(8,128)S(1)} fusion(f32[3072,512]{0,1:T(8,128)S(1)} %fusion.21, f32[512,512]{1,0:T(8,128)S(1)} %get-tuple-element.153), kind=kOutput, calls=%fused_computation.282 | convolution fusion | flops 9663676416 | bytes 13631488 | tf_op jit(solution)/shard_map/dot_general | solution.py:183
  884.5 12.4 %fusion.11 = f32[3072,512]{0,1:T(8,128)S(1)} fusion(f32[3072,512]{1,0:T(8,128)S(1)} %fusion.149, bf16[2048,1024]{1,0:T(8,128)(2,1)} %bitcast.182, bf16[1024,1024]{1,0:T(8,128)(2,1)S(1)} %copy-done.3, f32[128,512]{1,0:T(8,128)S(1)} %fusion.86, f32[128,512]{1,0:T(8,128)S(1)} %copy-done.12, f32[128,512]{1,0:T(8,128)S(1)} %copy-done.6, f32[128,512]{1,0:T(8,128)S(1)} %fusion.65), kind=kOutput, calls=%fused_computation.27 | convolution fusion | flops 9673900032 | bytes 19922944 | tf_op jit(solution)/shard_map/dot_general | solution.py:167
  897.0 30.5 %fusion.16 = f32[1024,2048]{0,1:T(8,128)} fusion(f32[1024,2048]{0,1:T(8,128)} %copy.60, f32[1,1024,1,2048]{1,3,2,0:T(8,128)S(1)} %bitcast.177, f32[3072,512]{0,1:T(8,128)S(1)} %fusion.11, f32[3072,512]{0,1:T(8,128)S(1)} %fusion.21), kind=kOutput, calls=%fused_computation.33 | convolution fusion | flops 25777143808 | bytes 37748736 | tf_op jit(solution)/shard_map/dot_general | solution.py:36
  936.3 20.5 %copy.73 = f32[1,1024,1,2048]{3,2,1,0:T(1,128)} copy(f32[1,1024,1,2048]{1,3,2,0:T(8,128)} %select_bitcast_fusion) | data formatting | bytes 16777216 | tf_op jit(solution)/shard_map/broadcast_in_dim | solution.py:196
  (210 shorter events, 236.7 us)
Async XLA Ops:
  6.5 20.5 %copy-start = (bf16[64,128,128]{2,1,0:T(8,128)(2,1)S(1)}, bf16[64,128,128]{2,1,0:T(8,128)(2,1)}, u32[]{:S(2)}) copy-start(bf16[64,128,128]{2,1,0:T(8,128)(2,1)} %param.23) | copy-start | bytes 6291460
  11.2 24.4 %all-to-all-start = ((s32[128,1,2]{2,1,0:T(1,128)}), s32[128,1,2]{2,1,0:T(1,128)S(1)}, u32[]{:S(2)}, u32[]{:S(2)}) async-start(s32[128,1,2]{2,1,0:T(1,128)} %bitcast.5), calls=%async_computation | async-start | bytes 131072 | tf_op jit(solution)/shard_map/all_to_all | solution.py:89
  35.6 20.7 %all-to-all-start.1 = ((s32[128,2,2,128]{3,1,2,0:T(2,128)}), s32[128,2,2,128]{3,1,2,0:T(2,128)S(1)}, u32[]{:S(2)}, u32[]{:S(2)}) async-start(s32[128,2,2,128]{3,1,2,0:T(2,128)} %pad_add_fusion), calls=%async_computation.1 | async-start | bytes 524288 | tf_op jit(solution)/shard_map/all_to_all | solution.py:82
  56.3 107.4 %all-to-all-start.2 = ((bf16[128,2,128,128]{3,2,1,0:T(8,128)(2,1)}), bf16[128,2,128,128]{3,2,1,0:T(8,128)(2,1)}, u32[]{:S(2)}, u32[]{:S(2)}) async-start(bf16[128,2,128,128]{3,2,1,0:T(8,128)(2,1)} %select_select_fusion), calls=%async_computation.2 | async-start | bytes 16777216 | tf_op jit(solution)/shard_map/all_to_all | solution.py:75
  63.0 446.6 %all-gather.3.cloned.1.call-start = ((), (), s32[]{:S(2)}) async-start(), calls=%async_computation.4 | async-start | bytes 4227072 | tf_op jit(solution)/shard_map/all_gather | solution.py:151
  254.2 2.0 copy-start.4
  292.1 53.1 %collective-permute-start.1 = (bf16[1024,1024]{0,1:T(8,128)(2,1)}, bf16[1024,1024]{0,1:T(8,128)(2,1)}, u32[]{:S(2)}, u32[]{:S(2)}) collective-permute-start(bf16[1024,1024]{0,1:T(8,128)(2,1)} %bitcast.20), channel_id=1, source_target_pairs={{0,0},{1,8},{2,16},{3,24},{4,32},{5,40},{6,48},{7,56},{8,1},{9,9},... | collective-permute-start | bytes 6291464 | tf_op jit(solution)/shard_map/ppermute | solution.py:138
  297.2 184.5 %collective-permute-start = (bf16[1024,1024]{0,1:T(8,128)(2,1)}, bf16[1024,1024]{0,1:T(8,128)(2,1)}, u32[]{:S(2)}, u32[]{:S(2)}) collective-permute-start(bf16[1024,1024]{0,1:T(8,128)(2,1)} %bitcast.20), channel_id=1, source_target_pairs={{0,64},{1,72},{2,80},{3,88},{4,96},{5,104},{6,112},{7,120},{8,65},... | collective-permute-start | bytes 6291464 | tf_op jit(solution)/shard_map/ppermute | solution.py:138
  522.0 1.9 copy-start.2
  526.4 1.0 copy-start.10
  669.1 9.6 copy-start.7
  669.1 9.6 copy-start.17
  671.0 11.9 %copy-start.13 = (f32[128,512]{1,0:T(8,128)}, f32[128,512]{1,0:T(8,128)S(1)}, u32[]{:S(2)}) copy-start(f32[128,512]{1,0:T(8,128)S(1)} %fusion.93) | copy-start | bytes 786436
  673.1 9.8 %copy-start.16 = (f32[128,512]{1,0:T(8,128)}, f32[128,512]{1,0:T(8,128)S(1)}, u32[]{:S(2)}) copy-start(f32[128,512]{1,0:T(8,128)S(1)} %fusion.92) | copy-start | bytes 786436
  688.7 1.0 copy-start.9
  714.8 0.7 copy-start.18
  740.2 0.7 copy-start.19
  791.1 64.8 %copy-start.8 = (f32[128,512]{1,0:T(8,128)S(1)}, f32[128,512]{1,0:T(8,128)}, u32[]{:S(2)}) copy-start(f32[128,512]{1,0:T(8,128)} %copy-done.7) | copy-start | bytes 786436
  791.1 64.8 %copy-start.14 = (f32[128,512]{1,0:T(8,128)S(1)}, f32[128,512]{1,0:T(8,128)}, u32[]{:S(2)}) copy-start(f32[128,512]{1,0:T(8,128)} %copy-done.13) | copy-start | bytes 786436
  846.6 0.7 copy-start.20
  850.2 5.6 copy-start.5
  852.9 2.9 copy-start.11
  862.9 21.5 %copy-start.3 = (bf16[1024,1024]{1,0:T(8,128)(2,1)S(1)}, bf16[1024,1024]{1,0:T(8,128)(2,1)}, u32[]{:S(2)}) copy-start(bf16[1024,1024]{1,0:T(8,128)(2,1)} %copy.63) | copy-start | bytes 6291460
  862.9 21.5 %copy-start.6 = (f32[128,512]{1,0:T(8,128)S(1)}, f32[128,512]{1,0:T(8,128)}, u32[]{:S(2)}) copy-start(f32[128,512]{1,0:T(8,128)} %copy-done.5) | copy-start | bytes 786436
  862.9 21.5 %copy-start.12 = (f32[128,512]{1,0:T(8,128)S(1)}, f32[128,512]{1,0:T(8,128)}, u32[]{:S(2)}) copy-start(f32[128,512]{1,0:T(8,128)} %copy-done.11) | copy-start | bytes 786436
  862.9 34.0 %slice-start = ((s8[8388608]{0:T(1024)(128)(4,1)}), s8[4194304]{0:T(1024)(128)(4,1)S(1)}, s32[]{:S(2)}) async-start(s8[8388608]{0:T(1024)(128)(4,1)} %bitcast.176), calls=%async_computation.5 | async-start | bytes 8388608
  884.5 12.4 %slice-start.1 = ((s8[8388608]{0:T(1024)(128)(4,1)}), s8[4194304]{0:T(1024)(128)(4,1)S(1)}, s32[]{:S(2)}) async-start(s8[8388608]{0:T(1024)(128)(4,1)} %bitcast.176), calls=%async_computation.6 | async-start | bytes 8388608
  897.0 30.6 %copy-start.15 = (f32[1024,128]{0,1:T(8,128)S(1)}, f32[1024,128]{0,1:T(8,128)}, u32[]{:S(2)}) copy-start(f32[1024,128]{0,1:T(8,128)} %copy.89) | copy-start | bytes 1572868
  897.0 30.5 %copy-start.21 = (pred[1024]{0:T(1024)(128)(4,1)S(1)}, pred[1024]{0:T(1024)(128)(4,1)}, u32[]{:S(2)}) copy-start(pred[1024]{0:T(1024)(128)(4,1)} %get-tuple-element.158) | copy-start | bytes 3076
  897.0 30.5 %copy-start.22 = (pred[1024]{0:T(1024)(128)(4,1)S(1)}, pred[1024]{0:T(1024)(128)(4,1)}, u32[]{:S(2)}) copy-start(pred[1024]{0:T(1024)(128)(4,1)} %get-tuple-element.159) | copy-start | bytes 3076
  930.3 26.4 %copy-start.1 = (bf16[64,128,128]{2,1,0:T(8,128)(2,1)S(1)}, bf16[64,128,128]{2,1,0:T(8,128)(2,1)}, u32[]{:S(2)}) copy-start(bf16[64,128,128]{2,1,0:T(8,128)(2,1)} %param.23) | copy-start | bytes 6291460
Sparse Core Ops, SparseCore 0:
  257.0 252.6 all-gather.2
